TPU v7x, 512 devices: a whole 4x4x16 slice. The times are simulated.
512 devices in a mesh: band: 16 (over x, y), lon: 32 (over z, core).
Axes of the slice: x: 4, y: 4, z: 16, core: 2. Of those that a mesh axis runs over, the one named last changes fastest.
Arguments:
- sky_maps: float32 [16, 8192, 256], P(None, ('band', 'lon')), may hold values from -9 to 9
- noise_var: float32 [8192, 256], P(('band', 'lon')), may hold values from 1 to 4
- position: float32 [3, 8192, 256], P(None, ('band', 'lon')), may hold values from -1 to 1
- leaf_basis: float32 [8192, 256, 64], P(('band', 'lon')), may hold values from -1 to 1
- leaf_couple: float32 [8192, 4, 64, 64], P(('band', 'lon')), as said below
- transfer: float32 [8192, 64, 64], P(('band', 'lon')), may hold values from -2 to 2
- panel_couple: float32 [1024, 2, 64, 64], P(('band', 'lon')), as said below
- near_list: int32 [8192, 5], P(('band', 'lon')), may hold values from -1 to 8191, as said below
- far_list: int32 [8192, 4], P(('band', 'lon')), may hold values from 0 to 8191, as said below
- panel_list: int32 [1024, 2], P(('band', 'lon')), may hold values from 0 to 1023, as said below
- leaf_panel: int32 [8192], P(('band', 'lon')), may hold values from 0 to 1
Outputs:
- solution: float32 [16, 8192, 256], P(None, ('band', 'lon'))
- residual: float32 [16, 8192, 256], P(None, ('band', 'lon'))
Inputs may be any that keep to these rules, and one draw needn't show every extreme that they name: `near_list`: entry 0 of a row is the leaf itself; the entries after it that are not -1 come first and are distinct leaves of the same band at cycle distance 1 or 2, the cycle closing; leaf j stands in leaf i's row exactly when i stands in j's. `far_list`: distinct leaves of the same band at cycle distance 3 to 6, the cycle closing; leaf j stands in leaf i's row exactly when i stands in j's. If leaf j stands in slot s of far_list[i] and leaf i in slot t of far_list[j], then leaf_couple[j, t] is the transpose of leaf_couple[i, s]. `panel_list`: entries are panel s of sectors of other bands at the same longitude (sector ids differing by a nonzero multiple of the sectors of a band), s being the panel's own index in its sector; panel j stands in panel k's row as often as k stands in j's. If panel j stands in slot s of panel_list[k] and these slots pair up with the slots t of panel_list[j] that hold k, then panel_couple[j, t] is the transpose of panel_couple[k, s].
All inputs are finite; a program needn't handle non-finite values.
Results may differ from a plain program's by a relative error of at most 0.0003.
Values sent between devices are 32-bit elements; how exact they have to be, the bound alone decides.
No kernel may reach another device: no remote copies, remote signals or barrier semaphores. Data moves between devices by JAX's collectives and lax.ppermute only.
A program may use at most 128 MiB of HBM per device.

v0:
```python
import math
import jax
import jax.numpy as jnp
from jax import lax
from jax.sharding import PartitionSpec as P

REACH = 6
ITERS = 2
HIGHEST_PRECISION = lax.Precision.HIGHEST
ROOT_THREE = math.sqrt(3.0)
AMPLITUDE = 0.02


def extended(cells, sides, width):
    for axis, dim in sides:
        count = lax.axis_size(axis)
        head = lax.slice_in_dim(cells, 0, width, axis=dim)
        tail = lax.slice_in_dim(cells, cells.shape[dim] - width, cells.shape[dim], axis=dim)
        cells = jnp.concatenate(
            [
                lax.ppermute(tail, axis, [(i, (i + 1) % count) for i in range(count)]),
                cells,
                lax.ppermute(head, axis, [((i + 1) % count, i) for i in range(count)]),
            ],
            axis=dim,
        )
    return cells


def all_sum(vector, axes):
    for axis in axes:
        count = lax.axis_size(axis)
        if count & count - 1:
            vector = lax.psum(vector, axis)
            continue
        stride = 1
        while stride < count:
            vector = vector + lax.ppermute(vector, axis, [(i, i ^ stride) for i in range(count)])
            stride *= 2
    return vector


def matern_block(rows_pos, cols_pos, length_scale):
    squared = jnp.zeros((cols_pos.shape[1], rows_pos.shape[1], cols_pos.shape[2]), jnp.float32)
    for component in range(3):
        offset = rows_pos[component][None, :, None] - cols_pos[component][:, None, :]
        squared = squared + offset * offset
    scaled = ROOT_THREE * jnp.sqrt(squared) / length_scale
    return AMPLITUDE * (1.0 + scaled) * jnp.exp(-scaled)


def on_device(
    sky_maps,
    noise_var,
    position,
    leaf_basis,
    leaf_couple,
    transfer,
    panel_couple,
    near_list,
    far_list,
    panel_list,
    leaf_panel,
):
    lon_index = lax.axis_index("lon")
    lon_count = lax.axis_size("lon")
    local_leaves = sky_maps.shape[1]
    pixel_count = sky_maps.shape[2]
    cycle_size = local_leaves * lon_count
    panel_count = panel_couple.shape[0]
    length_scale = 2.0 * math.pi / cycle_size
    first_leaf = lon_index * local_leaves
    near_depth = 2

    def rim_index(leaf_ids, depth):
        return (leaf_ids % cycle_size - first_leaf + depth) % cycle_size

    near_valid = near_list >= 0
    near_rows = rim_index(jnp.where(near_valid, near_list, near_list[:, :1]), near_depth)
    far_rows = rim_index(far_list, REACH)
    rim_pos = extended(position, (("lon", 1),), near_depth)

    def leaf_blocks(inputs):
        rows_pos, rows_index, slot_mask = inputs
        cols_pos = rim_pos[:, rows_index]
        return matern_block(rows_pos, cols_pos, length_scale) * slot_mask[:, None, None]

    near_blocks = jax.vmap(lambda *leaf: leaf_blocks(leaf))(
        jnp.transpose(position, (1, 0, 2)), near_rows, near_valid.astype(jnp.float32)
    )
    band_slot = panel_list // (lon_count * panel_count)
    gathered_rows = band_slot * panel_count + panel_list % panel_count
    membership = (leaf_panel[:, None] == jnp.arange(panel_count, dtype=jnp.int32)[None, :]).astype(
        jnp.float32
    )

    def square_total(vector):
        return all_sum(jnp.sum(vector * vector, axis=(1, 2)), ("lon", "band"))

    def covariance_apply(direction):
        coeffs = jnp.einsum("lpr,mlp->mlr", leaf_basis, direction, precision=HIGHEST_PRECISION)
        joined = jnp.concatenate([direction, coeffs], axis=2)
        rim_joined = extended(joined, (("lon", 1),), REACH)
        rim_values = rim_joined[
            :, REACH - near_depth : REACH + local_leaves + near_depth, :pixel_count
        ]
        rim_coeffs = rim_joined[:, :, pixel_count:]
        near_part = jnp.einsum(
            "lspq,mlsq->mlp", near_blocks, rim_values[:, near_rows], precision=HIGHEST_PRECISION
        )
        leaf_far = jnp.einsum(
            "lsab,mlsb->mla", leaf_couple, rim_coeffs[:, far_rows], precision=HIGHEST_PRECISION
        )
        upward = jnp.einsum("lab,mla->mlb", transfer, coeffs, precision=HIGHEST_PRECISION)
        panel_coeffs = jnp.einsum("lk,mlb->mkb", membership, upward, precision=HIGHEST_PRECISION)
        band_coeffs = lax.all_gather(panel_coeffs, "band", axis=1, tiled=True)
        panel_far = jnp.einsum(
            "ksab,mksb->mka",
            panel_couple,
            band_coeffs[:, gathered_rows],
            precision=HIGHEST_PRECISION,
        )
        downward = jnp.einsum("lk,mkb->mlb", membership, panel_far, precision=HIGHEST_PRECISION)
        leaf_far = leaf_far + jnp.einsum(
            "lab,mlb->mla", transfer, downward, precision=HIGHEST_PRECISION
        )
        far_part = jnp.einsum("lpr,mlr->mlp", leaf_basis, leaf_far, precision=HIGHEST_PRECISION)
        return noise_var[None] * direction + near_part + far_part

    solution = jnp.zeros_like(sky_maps)
    residual = sky_maps
    direction = sky_maps
    norm_now = square_total(residual)
    applied = covariance_apply(direction)
    for iteration in range(ITERS):
        curvature_sum = all_sum(jnp.sum(direction * applied, axis=(1, 2)), ("lon", "band"))
        step_size = norm_now / curvature_sum
        solution = solution + step_size[:, None, None] * direction
        residual = residual - step_size[:, None, None] * applied
        if iteration + 1 < ITERS:
            norm_next = square_total(residual)
            applied_residual = covariance_apply(residual)
            ratio = (norm_next / norm_now)[:, None, None]
            direction = residual + ratio * direction
            applied = applied_residual + ratio * applied
            norm_now = norm_next
    return (solution, residual)


def solution(mesh):
    placed = (
        P(None, ("band", "lon"), None),
        P(("band", "lon"), None),
        P(None, ("band", "lon"), None),
        P(("band", "lon"), None, None),
        P(("band", "lon"), None, None, None),
        P(("band", "lon"), None, None),
        P(("band", "lon"), None, None, None),
        P(("band", "lon"), None),
        P(("band", "lon"), None),
        P(("band", "lon"), None),
        P(("band", "lon")),
    )
    return jax.shard_map(
        on_device,
        mesh=mesh,
        in_specs=placed,
        out_specs=(P(None, ("band", "lon"), None), P(None, ("band", "lon"), None)),
        check_vma=False,
    )
```

profile of v0, /device:TPU:32, one launch (start us, length us, event | category | flops | bytes accessed | tf_op | source)
XLA Modules:
  0.0 391.8 jit_solution(15250787226746953187)
XLA Ops:
  2.5 1.9 collective-permute-start
  6.4 5.1 %collective-permute-start.12 = (f32[3,2,256]{2,0,1:T(4,128)}, f32[3,2,256]{2,0,1:T(4,128)}, u32[]{:S(2)}, u32[]{:S(2)}) collective-permute-start(f32[3,2,256]{2,0,1:T(4,128)} %get-tuple-element.24), channel_id=1, source_target_pairs={{1,0},{2,1},{3,2},{4,3},{5,4},{6,5},{7,6},{8,7},{9,8},{10,9},{11,1... | collective-permute-start | bytes 18440 | tf_op jit(solution)/shard_map/ppermute | solution.py:23
  12.6 2.4 convolution_bitcast_fusion.9
  21.0 20.7 %all_gather.6 = f32[16,32,64]{2,0,1:T(8,128)S(1)} all-gather(f32[16,2,64]{2,0,1:T(8,128)S(1)} %copy.55), channel_id=1, replica_groups=mesh['band'=16,'lon'=32] {'band'}, dimensions={1}, use_global_device_ids=true | all-gather | bytes 139264 | tf_op jit(solution)/shard_map/all_gather | solution.py:116
  44.9 10.6 %collective-permute-start.1 = (f32[16]{0:T(128)S(1)}, f32[16]{0:T(128)S(1)}, u32[]{:S(2)}, u32[]{:S(2)}) collective-permute-start(f32[16]{0:T(128)S(1)} %add.208), channel_id=1, source_target_pairs={{0,2},{1,3},{2,0},{3,1},{4,6},{5,7},{6,4},{7,5},{8,10},{9,11},{10,... | collective-permute-start | bytes 200 | tf_op jit(solution)/shard_map/ppermute | solution.py:38
  59.5 3.8 collective-permute-done.2
  63.3 2.5 collective-permute-start.3
  67.1 5.5 %collective-permute-done.3 = f32[16]{0:T(128)S(1)} collective-permute-done((f32[16]{0:T(128)S(1)}, f32[16]{0:T(128)S(1)}, u32[]{:S(2)}, u32[]{:S(2)}) %collective-permute-start.3) | collective-permute-done | bytes 96 | tf_op jit(solution)/shard_map/ppermute | solution.py:38
  73.2 9.1 %collective-permute-start.4 = (f32[16]{0:T(128)}, f32[16]{0:T(128)}, u32[]{:S(2)}, u32[]{:S(2)}) collective-permute-start(f32[16]{0:T(128)} %add.211), channel_id=1, source_target_pairs={{0,16},{1,17},{2,18},{3,19},{4,20},{5,21},{6,22},{7,23},{8,24},{9,... | collective-permute-start | bytes 200 | tf_op jit(solution)/shard_map/ppermute | solution.py:38
  90.0 3.0 convolution_bitcast_fusion.7
  94.0 32.2 %fusion.27 = f32[16,16,256]{2,0,1:T(8,128)S(1)} fusion(f32[16,16,5,256]{3,0,2,1:T(8,128)S(1)} %bitcast.127, f32[16,5]{1,0:T(8,128)S(1)} %copy-done.39, f32[16,5,256]{2,1,0:T(8,128)S(1)} %copy-done.26, f32[16,256]{1,0:T(8,128)S(1)} %copy-done.32, f32[16,5,256]{2,1,0:T(8,128)S(1)} %copy-done.25, f32[16,256]{1,0:T(8,128)S(1)} %copy-done.34, ...), kind=kOutput, calls=%fused_computation.37 | convolution fusion | flops 1080164352 | bytes 2146624 | tf_op jit(solution)/shard_map/lspq,mlsq->mlp/dot_general | solution.py:108
  127.1 1.9 collective-permute-start.13
  130.1 3.9 collective-permute-start.14
  134.1 3.1 collective-permute-start.5
  137.2 1.9 collective-permute-start.15
  139.5 4.0 %collective-permute-done.15 = f32[16]{0:T(128)S(1)} collective-permute-done((f32[16]{0:T(128)S(1)}, f32[16]{0:T(128)S(1)}, u32[]{:S(2)}, u32[]{:S(2)}) %collective-permute-start.15) | collective-permute-done | bytes 96 | tf_op jit(solution)/shard_map/ppermute | solution.py:38
  143.5 4.3 %collective-permute-start.16 = (f32[16]{0:T(128)S(1)}, f32[16]{0:T(128)S(1)}, u32[]{:S(2)}, u32[]{:S(2)}) collective-permute-start(f32[16]{0:T(128)S(1)} %add.240), channel_id=1, source_target_pairs={{0,8},{1,9},{2,10},{3,11},{4,12},{5,13},{6,14},{7,15},{8,0},{9,1},... | collective-permute-start | bytes 200 | tf_op jit(solution)/shard_map/ppermute | solution.py:38
  147.8 4.6 %collective-permute-start.6 = (f32[16]{0:T(128)S(1)}, f32[16]{0:T(128)S(1)}, u32[]{:S(2)}, u32[]{:S(2)}) collective-permute-start(f32[16]{0:T(128)S(1)} %add.213), channel_id=1, source_target_pairs={{0,64},{32,96},{64,0},{96,32},{128,192},{160,224},{192,128},{224,1... | collective-permute-start | bytes 200 | tf_op jit(solution)/shard_map/ppermute | solution.py:38
  152.9 5.5 %collective-permute-start.17 = (f32[16]{0:T(128)S(1)}, f32[16]{0:T(128)S(1)}, u32[]{:S(2)}, u32[]{:S(2)}) collective-permute-start(f32[16]{0:T(128)S(1)} %add.241), channel_id=1, source_target_pairs={{0,16},{1,17},{2,18},{3,19},{4,20},{5,21},{6,22},{7,23},{8,24},{9,... | collective-permute-start | bytes 200 | tf_op jit(solution)/shard_map/ppermute | solution.py:38
  158.4 8.6 %collective-permute-done.17 = f32[16]{0:T(128)S(1)} collective-permute-done((f32[16]{0:T(128)S(1)}, f32[16]{0:T(128)S(1)}, u32[]{:S(2)}, u32[]{:S(2)}) %collective-permute-start.17) | collective-permute-done | bytes 96 | tf_op jit(solution)/shard_map/ppermute | solution.py:38
  167.0 2.7 collective-permute-start.18
  169.7 3.1 collective-permute-start.7
  172.9 4.1 %collective-permute-start.19 = (f32[16]{0:T(128)S(1)}, f32[16]{0:T(128)S(1)}, u32[]{:S(2)}, u32[]{:S(2)}) collective-permute-start(f32[16]{0:T(128)S(1)} %add.243), channel_id=1, source_target_pairs={{0,64},{32,96},{64,0},{96,32},{128,192},{160,224},{192,128},{224,1... | collective-permute-start | bytes 200 | tf_op jit(solution)/shard_map/ppermute | solution.py:38
  177.0 2.8 collective-permute-done.19
  179.8 2.7 collective-permute-start.20
  182.6 4.6 %collective-permute-start.8 = (f32[16]{0:T(128)S(1)}, f32[16]{0:T(128)S(1)}, u32[]{:S(2)}, u32[]{:S(2)}) collective-permute-start(f32[16]{0:T(128)S(1)} %add.215), channel_id=1, source_target_pairs={{0,256},{32,288},{64,320},{96,352},{128,384},{160,416},{192,448},{... | collective-permute-start | bytes 200 | tf_op jit(solution)/shard_map/ppermute | solution.py:38
  187.2 2.8 collective-permute-start.21
  190.0 4.1 %collective-permute-done.21 = f32[16]{0:T(128)S(1)} collective-permute-done((f32[16]{0:T(128)S(1)}, f32[16]{0:T(128)S(1)}, u32[]{:S(2)}, u32[]{:S(2)}) %collective-permute-start.21) | collective-permute-done | bytes 96 | tf_op jit(solution)/shard_map/ppermute | solution.py:38
  194.9 1.9 collective-permute-start.22
  198.6 2.2 collective-permute-start.23
  200.8 3.2 collective-permute-done.23
  204.0 1.9 collective-permute-start.24
  206.0 24.0 %all_gather.7 = f32[16,32,64]{2,0,1:T(8,128)} all-gather(f32[16,2,64]{2,0,1:T(8,128)S(1)} %copy.63), channel_id=1, replica_groups=mesh['band'=16,'lon'=32] {'band'}, dimensions={1}, use_global_device_ids=true | all-gather | bytes 139264 | tf_op jit(solution)/shard_map/all_gather | solution.py:116
  229.9 4.6 %collective-permute-start.25 = (f32[16]{0:T(128)S(1)}, f32[16]{0:T(128)}, u32[]{:S(2)}, u32[]{:S(2)}) collective-permute-start(f32[16]{0:T(128)S(1)} %add.249), channel_id=1, source_target_pairs={{0,8},{1,9},{2,10},{3,11},{4,12},{5,13},{6,14},{7,15},{8,0},{9,1},... | collective-permute-start | bytes 200 | tf_op jit(solution)/shard_map/ppermute | solution.py:38
  234.5 2.2 gather_fusion.6
  236.8 2.5 collective-permute-done.25
  239.9 5.5 %collective-permute-start.26 = (f32[16]{0:T(128)S(1)}, f32[16]{0:T(128)S(1)}, u32[]{:S(2)}, u32[]{:S(2)}) collective-permute-start(f32[16]{0:T(128)S(1)} %add.250), channel_id=1, source_target_pairs={{0,16},{1,17},{2,18},{3,19},{4,20},{5,21},{6,22},{7,23},{8,24},{9,... | collective-permute-start | bytes 200 | tf_op jit(solution)/shard_map/ppermute | solution.py:38
  246.5 7.5 %collective-permute-done.26 = f32[16]{0:T(128)S(1)} collective-permute-done((f32[16]{0:T(128)S(1)}, f32[16]{0:T(128)S(1)}, u32[]{:S(2)}, u32[]{:S(2)}) %collective-permute-start.26) | collective-permute-done | bytes 96 | tf_op jit(solution)/shard_map/ppermute | solution.py:38
  254.1 2.7 collective-permute-start.27
  259.5 4.1 %collective-permute-start.28 = (f32[16]{0:T(128)S(1)}, f32[16]{0:T(128)S(1)}, u32[]{:S(2)}, u32[]{:S(2)}) collective-permute-start(f32[16]{0:T(128)S(1)} %add.252), channel_id=1, source_target_pairs={{0,64},{32,96},{64,0},{96,32},{128,192},{160,224},{192,128},{224,1... | collective-permute-start | bytes 200 | tf_op jit(solution)/shard_map/ppermute | solution.py:38
  263.6 2.8 collective-permute-done.28
  266.4 2.7 collective-permute-start.29
  269.2 2.7 collective-permute-done.29
  271.8 4.0 %collective-permute-start.30 = (f32[16]{0:T(128)S(1)}, f32[16]{0:T(128)S(1)}, u32[]{:S(2)}, u32[]{:S(2)}) collective-permute-start(f32[16]{0:T(128)S(1)} %add.254), channel_id=1, source_target_pairs={{0,256},{32,288},{64,320},{96,352},{128,384},{160,416},{192,448},{... | collective-permute-start | bytes 200 | tf_op jit(solution)/shard_map/ppermute | solution.py:38
  275.8 2.9 collective-permute-done.30
  281.4 2.3 gather_fusion.5
  283.8 3.6 convolution_bitcast_fusion.4
  290.2 34.7 %fusion.26 = f32[16,16,256]{2,0,1:T(8,128)S(1)} fusion(f32[16,16,5,256]{3,0,2,1:T(8,128)} %bitcast.128, f32[16,5]{1,0:T(8,128)S(1)} %copy-done.40, f32[16,5,256]{2,1,0:T(8,128)} %get-tuple-element.18, f32[16,256]{1,0:T(8,128)S(1)} %copy-done.33, f32[16,5,256]{2,1,0:T(8,128)} %get-tuple-element.17, f32[16,256]{1,0:T(8,128)S(1)} %copy-done.35, ...), kind=kOutput, calls=%fused_computation.36 | convolution fusion | flops 1080164352 | bytes 2146624 | tf_op jit(solution)/shard_map/lspq,mlsq->mlp/dot_general | solution.py:108
  326.7 2.4 collective-permute-start.33
  329.9 2.2 collective-permute-start.34
  332.1 3.2 collective-permute-done.34
  335.3 4.7 %collective-permute-start.35 = (f32[16]{0:T(128)S(1)}, f32[16]{0:T(128)S(1)}, u32[]{:S(2)}, u32[]{:S(2)}) collective-permute-start(f32[16]{0:T(128)S(1)} %add.263), channel_id=1, source_target_pairs={{0,4},{1,5},{2,6},{3,7},{4,0},{5,1},{6,2},{7,3},{8,12},{9,13},{10,... | collective-permute-start | bytes 200 | tf_op jit(solution)/shard_map/ppermute | solution.py:38
  341.6 4.4 %collective-permute-start.36 = (f32[16]{0:T(128)S(1)}, f32[16]{0:T(128)S(1)}, u32[]{:S(2)}, u32[]{:S(2)}) collective-permute-start(f32[16]{0:T(128)S(1)} %add.264), channel_id=1, source_target_pairs={{0,8},{1,9},{2,10},{3,11},{4,12},{5,13},{6,14},{7,15},{8,0},{9,1},... | collective-permute-start | bytes 200 | tf_op jit(solution)/shard_map/ppermute | solution.py:38
  346.0 4.9 %collective-permute-done.36 = f32[16]{0:T(128)S(1)} collective-permute-done((f32[16]{0:T(128)S(1)}, f32[16]{0:T(128)S(1)}, u32[]{:S(2)}, u32[]{:S(2)}) %collective-permute-start.36) | collective-permute-done | bytes 96 | tf_op jit(solution)/shard_map/ppermute | solution.py:38
  350.9 5.5 %collective-permute-start.37 = (f32[16]{0:T(128)S(1)}, f32[16]{0:T(128)S(1)}, u32[]{:S(2)}, u32[]{:S(2)}) collective-permute-start(f32[16]{0:T(128)S(1)} %add.265), channel_id=1, source_target_pairs={{0,16},{1,17},{2,18},{3,19},{4,20},{5,21},{6,22},{7,23},{8,24},{9,... | collective-permute-start | bytes 200 | tf_op jit(solution)/shard_map/ppermute | solution.py:38
  356.4 8.7 %collective-permute-done.37 = f32[16]{0:T(128)S(1)} collective-permute-done((f32[16]{0:T(128)S(1)}, f32[16]{0:T(128)S(1)}, u32[]{:S(2)}, u32[]{:S(2)}) %collective-permute-start.37) | collective-permute-done | bytes 96 | tf_op jit(solution)/shard_map/ppermute | solution.py:38
  365.1 2.6 collective-permute-start.38
  367.7 2.8 collective-permute-done.38
  370.5 3.9 %collective-permute-start.39 = (f32[16]{0:T(128)S(1)}, f32[16]{0:T(128)S(1)}, u32[]{:S(2)}, u32[]{:S(2)}) collective-permute-start(f32[16]{0:T(128)S(1)} %add.267), channel_id=1, source_target_pairs={{0,64},{32,96},{64,0},{96,32},{128,192},{160,224},{192,128},{224,1... | collective-permute-start | bytes 200 | tf_op jit(solution)/shard_map/ppermute | solution.py:38
  374.5 3.0 collective-permute-done.39
  377.4 2.7 collective-permute-start.40
  380.2 2.7 collective-permute-done.40
  382.9 3.8 collective-permute-start.41
  386.7 3.1 collective-permute-done.41
  (204 shorter events, 50.1 us)
Async XLA Ops:
  0.6 89.4 %copy-start = (f32[16,4,64,64]{3,2,1,0:T(8,128)S(1)}, f32[16,4,64,64]{3,2,1,0:T(8,128)}, u32[]{:S(2)}) copy-start(f32[16,4,64,64]{3,2,1,0:T(8,128)} %param.15) | copy-start | bytes 3145732
  0.6 19.0 %copy-start.23 = (f32[3,16,256]{2,1,0:T(8,128)S(1)}, f32[3,16,256]{2,1,0:T(8,128)}, u32[]{:S(2)}) copy-start(f32[3,16,256]{2,1,0:T(8,128)} %param.13) | copy-start | bytes 147460
  0.7 16.8 %copy-start.29 = (s32[16,5]{0,1:T(8,128)S(1)}, s32[16,5]{0,1:T(8,128)}, u32[]{:S(2)}) copy-start(s32[16,5]{0,1:T(8,128)} %param.18) | copy-start | bytes 964
  0.7 17.4 %copy-start.42 = (s32[2,2]{1,0:T(2,128)S(1)}, s32[2,2]{1,0:T(2,128)}, u32[]{:S(2)}) copy-start(s32[2,2]{1,0:T(2,128)} %param.20) | copy-start | bytes 52
  0.7 17.5 %copy-start.41 = (s32[16,4]{0,1:T(4,128)S(1)}, s32[16,4]{0,1:T(4,128)}, u32[]{:S(2)}) copy-start(s32[16,4]{0,1:T(4,128)} %param.19) | copy-start | bytes 772
  0.7 19.5 %copy-start.6 = (f32[16,64,64]{2,1,0:T(8,128)S(1)}, f32[16,64,64]{2,1,0:T(8,128)}, u32[]{:S(2)}) copy-start(f32[16,64,64]{2,1,0:T(8,128)} %param.16) | copy-start | bytes 786436
  0.7 20.1 %copy-start.37 = (s32[16]{0:T(128)S(1)}, s32[16]{0:T(128)}, u32[]{:S(2)}) copy-start(s32[16]{0:T(128)} %param.21) | copy-start | bytes 196
  2.5 41.7 %collective-permute-start = (f32[16]{0:T(128)}, f32[16]{0:T(128)}, u32[]{:S(2)}, u32[]{:S(2)}) collective-permute-start(f32[16]{0:T(128)} %multiply_reduce_fusion.3), channel_id=1, source_target_pairs={{0,1},{1,0},{2,3},{3,2},{4,5},{5,4},{6,7},{7,6},{8,9},{9,8},{10,11... | collective-permute-start | bytes 200 | tf_op jit(solution)/shard_map/ppermute | solution.py:38
  5.3 37.0 %copy-start.19 = (f32[2,2,64,64]{3,2,1,0:T(8,128)S(1)}, f32[2,2,64,64]{3,2,1,0:T(8,128)}, u32[]{:S(2)}) copy-start(f32[2,2,64,64]{3,2,1,0:T(8,128)} %param.17) | copy-start | bytes 196612
  5.9 76.4 %collective-permute-start.11 = (f32[3,2,256]{2,0,1:T(4,128)}, f32[3,2,256]{2,0,1:T(4,128)}, u32[]{:S(2)}, u32[]{:S(2)}) collective-permute-start(f32[3,2,256]{2,0,1:T(4,128)} %get-tuple-element.23), channel_id=1, source_target_pairs={{0,1},{1,2},{2,3},{3,4},{4,5},{5,6},{6,7},{7,8},{8,9},{9,10},{10,1... | collective-permute-start | bytes 18440 | tf_op jit(solution)/shard_map/ppermute | solution.py:21
  6.4 75.9 %collective-permute-start.12 = (f32[3,2,256]{2,0,1:T(4,128)}, f32[3,2,256]{2,0,1:T(4,128)}, u32[]{:S(2)}, u32[]{:S(2)}) collective-permute-start(f32[3,2,256]{2,0,1:T(4,128)} %get-tuple-element.24), channel_id=1, source_target_pairs={{1,0},{2,1},{3,2},{4,3},{5,4},{6,5},{7,6},{8,7},{9,8},{10,9},{11,1... | collective-permute-start | bytes 18440 | tf_op jit(solution)/shard_map/ppermute | solution.py:23
  15.7 69.2 %collective-permute-start.9 = (f32[16,6,320]{2,0,1:T(8,128)}, f32[16,6,320]{2,0,1:T(8,128)}, u32[]{:S(2)}, u32[]{:S(2)}) collective-permute-start(f32[16,6,320]{2,0,1:T(8,128)} %get-tuple-element.19), channel_id=1, source_target_pairs={{0,1},{1,2},{2,3},{3,4},{4,5},{5,6},{6,7},{7,8},{8,9},{9,10},{10,1... | collective-permute-start | bytes 368648 | tf_op jit(solution)/shard_map/ppermute | solution.py:21
  15.7 69.2 %collective-permute-start.10 = (f32[16,6,320]{2,0,1:T(8,128)}, f32[16,6,320]{2,0,1:T(8,128)}, u32[]{:S(2)}, u32[]{:S(2)}) collective-permute-start(f32[16,6,320]{2,0,1:T(8,128)} %get-tuple-element.20), channel_id=1, source_target_pairs={{1,0},{2,1},{3,2},{4,3},{5,4},{6,5},{7,6},{8,7},{9,8},{10,9},{11,1... | collective-permute-start | bytes 368648 | tf_op jit(solution)/shard_map/ppermute | solution.py:23
  18.8 23.4 %copy-start.36 = (s32[1024]{0:T(1024)}, s32[1024]{0:T(1024)S(1)}, u32[]{:S(2)}) copy-start(s32[1024]{0:T(1024)S(1)} %pad_clamp_fusion) | copy-start | bytes 12292
  44.9 12.1 %collective-permute-start.1 = (f32[16]{0:T(128)S(1)}, f32[16]{0:T(128)S(1)}, u32[]{:S(2)}, u32[]{:S(2)}) collective-permute-start(f32[16]{0:T(128)S(1)} %add.208), channel_id=1, source_target_pairs={{0,2},{1,3},{2,0},{3,1},{4,6},{5,7},{6,4},{7,5},{8,10},{9,11},{10,... | collective-permute-start | bytes 200 | tf_op jit(solution)/shard_map/ppermute | solution.py:38
  57.0 6.3 %collective-permute-start.2 = (f32[16]{0:T(128)S(1)}, f32[16]{0:T(128)S(1)}, u32[]{:S(2)}, u32[]{:S(2)}) collective-permute-start(f32[16]{0:T(128)S(1)} %add.209), channel_id=1, source_target_pairs={{0,4},{1,5},{2,6},{3,7},{4,0},{5,1},{6,2},{7,3},{8,12},{9,13},{10,... | collective-permute-start | bytes 200 | tf_op jit(solution)/shard_map/ppermute | solution.py:38
  63.3 9.3 %collective-permute-start.3 = (f32[16]{0:T(128)S(1)}, f32[16]{0:T(128)S(1)}, u32[]{:S(2)}, u32[]{:S(2)}) collective-permute-start(f32[16]{0:T(128)S(1)} %add.210), channel_id=1, source_target_pairs={{0,8},{1,9},{2,10},{3,11},{4,12},{5,13},{6,14},{7,15},{8,0},{9,1},... | collective-permute-start | bytes 200 | tf_op jit(solution)/shard_map/ppermute | solution.py:38
  73.2 55.8 %collective-permute-start.4 = (f32[16]{0:T(128)}, f32[16]{0:T(128)}, u32[]{:S(2)}, u32[]{:S(2)}) collective-permute-start(f32[16]{0:T(128)} %add.211), channel_id=1, source_target_pairs={{0,16},{1,17},{2,18},{3,19},{4,20},{5,21},{6,22},{7,23},{8,24},{9,... | collective-permute-start | bytes 200 | tf_op jit(solution)/shard_map/ppermute | solution.py:38
  94.0 32.3 %copy-start.1 = (f32[16,256,64]{1,2,0:T(8,128)S(1)}, f32[16,256,64]{1,2,0:T(8,128)}, u32[]{:S(2)}) copy-start(f32[16,256,64]{1,2,0:T(8,128)} %param.14) | copy-start | bytes 3145732
  126.3 71.5 %copy-start.7 = (f32[16,64,64]{2,1,0:T(8,128)S(1)}, f32[16,64,64]{2,1,0:T(8,128)}, u32[]{:S(2)}) copy-start(f32[16,64,64]{2,1,0:T(8,128)} %param.16) | copy-start | bytes 786436
  126.3 72.1 %copy-start.38 = (s32[16]{0:T(128)S(1)}, s32[16]{0:T(128)}, u32[]{:S(2)}) copy-start(s32[16]{0:T(128)} %param.21) | copy-start | bytes 196
  127.1 71.3 %copy-start.9 = (f32[16,16,256]{2,0,1:T(8,128)}, f32[16,16,256]{2,0,1:T(8,128)S(1)}, u32[]{:S(2)}) copy-start(f32[16,16,256]{2,0,1:T(8,128)S(1)} %get-tuple-element.29) | copy-start | bytes 786436
  127.1 3.0 collective-permute-start.13
  130.1 7.0 %collective-permute-start.14 = (f32[16]{0:T(128)S(1)}, f32[16]{0:T(128)S(1)}, u32[]{:S(2)}, u32[]{:S(2)}) collective-permute-start(f32[16]{0:T(128)S(1)} %add.238), channel_id=1, source_target_pairs={{0,2},{1,3},{2,0},{3,1},{4,6},{5,7},{6,4},{7,5},{8,10},{9,11},{10,... | collective-permute-start | bytes 200 | tf_op jit(solution)/shard_map/ppermute | solution.py:38
  134.1 5.4 %collective-permute-start.5 = (f32[16]{0:T(128)S(1)}, f32[16]{0:T(128)S(1)}, u32[]{:S(2)}, u32[]{:S(2)}) collective-permute-start(f32[16]{0:T(128)S(1)} %add.212), channel_id=1, source_target_pairs={{0,32},{32,0},{64,96},{96,64},{128,160},{160,128},{192,224},{224,1... | collective-permute-start | bytes 200 | tf_op jit(solution)/shard_map/ppermute | solution.py:38
  137.2 6.3 %collective-permute-start.15 = (f32[16]{0:T(128)S(1)}, f32[16]{0:T(128)S(1)}, u32[]{:S(2)}, u32[]{:S(2)}) collective-permute-start(f32[16]{0:T(128)S(1)} %add.239), channel_id=1, source_target_pairs={{0,4},{1,5},{2,6},{3,7},{4,0},{5,1},{6,2},{7,3},{8,12},{9,13},{10,... | collective-permute-start | bytes 200 | tf_op jit(solution)/shard_map/ppermute | solution.py:38
  143.5 9.3 %collective-permute-start.16 = (f32[16]{0:T(128)S(1)}, f32[16]{0:T(128)S(1)}, u32[]{:S(2)}, u32[]{:S(2)}) collective-permute-start(f32[16]{0:T(128)S(1)} %add.240), channel_id=1, source_target_pairs={{0,8},{1,9},{2,10},{3,11},{4,12},{5,13},{6,14},{7,15},{8,0},{9,1},... | collective-permute-start | bytes 200 | tf_op jit(solution)/shard_map/ppermute | solution.py:38
  147.8 10.5 %collective-permute-start.6 = (f32[16]{0:T(128)S(1)}, f32[16]{0:T(128)S(1)}, u32[]{:S(2)}, u32[]{:S(2)}) collective-permute-start(f32[16]{0:T(128)S(1)} %add.213), channel_id=1, source_target_pairs={{0,64},{32,96},{64,0},{96,32},{128,192},{160,224},{192,128},{224,1... | collective-permute-start | bytes 200 | tf_op jit(solution)/shard_map/ppermute | solution.py:38
  152.9 14.1 %collective-permute-start.17 = (f32[16]{0:T(128)S(1)}, f32[16]{0:T(128)S(1)}, u32[]{:S(2)}, u32[]{:S(2)}) collective-permute-start(f32[16]{0:T(128)S(1)} %add.241), channel_id=1, source_target_pairs={{0,16},{1,17},{2,18},{3,19},{4,20},{5,21},{6,22},{7,23},{8,24},{9,... | collective-permute-start | bytes 200 | tf_op jit(solution)/shard_map/ppermute | solution.py:38
  167.0 5.8 %collective-permute-start.18 = (f32[16]{0:T(128)S(1)}, f32[16]{0:T(128)S(1)}, u32[]{:S(2)}, u32[]{:S(2)}) collective-permute-start(f32[16]{0:T(128)S(1)} %add.242), channel_id=1, source_target_pairs={{0,32},{32,0},{64,96},{96,64},{128,160},{160,128},{192,224},{224,1... | collective-permute-start | bytes 200 | tf_op jit(solution)/shard_map/ppermute | solution.py:38
  169.7 7.3 %collective-permute-start.7 = (f32[16]{0:T(128)S(1)}, f32[16]{0:T(128)S(1)}, u32[]{:S(2)}, u32[]{:S(2)}) collective-permute-start(f32[16]{0:T(128)S(1)} %add.214), channel_id=1, source_target_pairs={{0,128},{32,160},{64,192},{96,224},{128,0},{160,32},{192,64},{224,... | collective-permute-start | bytes 200 | tf_op jit(solution)/shard_map/ppermute | solution.py:38
  172.9 6.9 %collective-permute-start.19 = (f32[16]{0:T(128)S(1)}, f32[16]{0:T(128)S(1)}, u32[]{:S(2)}, u32[]{:S(2)}) collective-permute-start(f32[16]{0:T(128)S(1)} %add.243), channel_id=1, source_target_pairs={{0,64},{32,96},{64,0},{96,32},{128,192},{160,224},{192,128},{224,1... | collective-permute-start | bytes 200 | tf_op jit(solution)/shard_map/ppermute | solution.py:38
  179.8 7.3 %collective-permute-start.20 = (f32[16]{0:T(128)S(1)}, f32[16]{0:T(128)S(1)}, u32[]{:S(2)}, u32[]{:S(2)}) collective-permute-start(f32[16]{0:T(128)S(1)} %add.244), channel_id=1, source_target_pairs={{0,128},{32,160},{64,192},{96,224},{128,0},{160,32},{192,64},{224,... | collective-permute-start | bytes 200 | tf_op jit(solution)/shard_map/ppermute | solution.py:38
  182.6 7.4 %collective-permute-start.8 = (f32[16]{0:T(128)S(1)}, f32[16]{0:T(128)S(1)}, u32[]{:S(2)}, u32[]{:S(2)}) collective-permute-start(f32[16]{0:T(128)S(1)} %add.215), channel_id=1, source_target_pairs={{0,256},{32,288},{64,320},{96,352},{128,384},{160,416},{192,448},{... | collective-permute-start | bytes 200 | tf_op jit(solution)/shard_map/ppermute | solution.py:38
  187.2 6.9 %collective-permute-start.21 = (f32[16]{0:T(128)S(1)}, f32[16]{0:T(128)S(1)}, u32[]{:S(2)}, u32[]{:S(2)}) collective-permute-start(f32[16]{0:T(128)S(1)} %add.245), channel_id=1, source_target_pairs={{0,256},{32,288},{64,320},{96,352},{128,384},{160,416},{192,448},{... | collective-permute-start | bytes 200 | tf_op jit(solution)/shard_map/ppermute | solution.py:38
  194.9 88.8 %copy-start.4 = (f32[16,16,256]{2,0,1:T(8,128)}, f32[16,16,256]{2,0,1:T(8,128)S(1)}, u32[]{:S(2)}) copy-start(f32[16,16,256]{2,0,1:T(8,128)S(1)} %get-tuple-element.11) | copy-start | bytes 786436
  194.9 3.7 collective-permute-start.22
  196.8 84.6 %copy-start.28 = (s32[1024]{0:T(1024)S(1)}, s32[1024]{0:T(1024)}, u32[]{:S(2)}) copy-start(s32[1024]{0:T(1024)} %pad_clamp_fusion.1) | copy-start | bytes 12292
  197.8 85.9 %copy-start.12 = (f32[16,16,64]{2,0,1:T(8,128)}, f32[16,16,64]{2,0,1:T(8,128)S(1)}, u32[]{:S(2)}) copy-start(f32[16,16,64]{2,0,1:T(8,128)S(1)} %convolution_bitcast_fusion.8) | copy-start | bytes 196612
  198.6 5.4 %collective-permute-start.23 = (f32[16]{0:T(128)S(1)}, f32[16]{0:T(128)S(1)}, u32[]{:S(2)}, u32[]{:S(2)}) collective-permute-start(f32[16]{0:T(128)S(1)} %add.247), channel_id=1, source_target_pairs={{0,2},{1,3},{2,0},{3,1},{4,6},{5,7},{6,4},{7,5},{8,10},{9,11},{10,... | collective-permute-start | bytes 200 | tf_op jit(solution)/shard_map/ppermute | solution.py:38
  204.0 25.9 %collective-permute-start.24 = (f32[16]{0:T(128)S(1)}, f32[16]{0:T(128)S(1)}, u32[]{:S(2)}, u32[]{:S(2)}) collective-permute-start(f32[16]{0:T(128)S(1)} %add.248), channel_id=1, source_target_pairs={{0,4},{1,5},{2,6},{3,7},{4,0},{5,1},{6,2},{7,3},{8,12},{9,13},{10,... | collective-permute-start | bytes 200 | tf_op jit(solution)/shard_map/ppermute | solution.py:38
  229.9 9.3 %collective-permute-start.25 = (f32[16]{0:T(128)S(1)}, f32[16]{0:T(128)}, u32[]{:S(2)}, u32[]{:S(2)}) collective-permute-start(f32[16]{0:T(128)S(1)} %add.249), channel_id=1, source_target_pairs={{0,8},{1,9},{2,10},{3,11},{4,12},{5,13},{6,14},{7,15},{8,0},{9,1},... | collective-permute-start | bytes 200 | tf_op jit(solution)/shard_map/ppermute | solution.py:38
  239.9 14.1 %collective-permute-start.26 = (f32[16]{0:T(128)S(1)}, f32[16]{0:T(128)S(1)}, u32[]{:S(2)}, u32[]{:S(2)}) collective-permute-start(f32[16]{0:T(128)S(1)} %add.250), channel_id=1, source_target_pairs={{0,16},{1,17},{2,18},{3,19},{4,20},{5,21},{6,22},{7,23},{8,24},{9,... | collective-permute-start | bytes 200 | tf_op jit(solution)/shard_map/ppermute | solution.py:38
  254.1 5.4 %collective-permute-start.27 = (f32[16]{0:T(128)S(1)}, f32[16]{0:T(128)S(1)}, u32[]{:S(2)}, u32[]{:S(2)}) collective-permute-start(f32[16]{0:T(128)S(1)} %add.251), channel_id=1, source_target_pairs={{0,32},{32,0},{64,96},{96,64},{128,160},{160,128},{192,224},{224,1... | collective-permute-start | bytes 200 | tf_op jit(solution)/shard_map/ppermute | solution.py:38
  259.5 6.9 %collective-permute-start.28 = (f32[16]{0:T(128)S(1)}, f32[16]{0:T(128)S(1)}, u32[]{:S(2)}, u32[]{:S(2)}) collective-permute-start(f32[16]{0:T(128)S(1)} %add.252), channel_id=1, source_target_pairs={{0,64},{32,96},{64,0},{96,32},{128,192},{160,224},{192,128},{224,1... | collective-permute-start | bytes 200 | tf_op jit(solution)/shard_map/ppermute | solution.py:38
  266.4 5.4 %collective-permute-start.29 = (f32[16]{0:T(128)S(1)}, f32[16]{0:T(128)S(1)}, u32[]{:S(2)}, u32[]{:S(2)}) collective-permute-start(f32[16]{0:T(128)S(1)} %add.253), channel_id=1, source_target_pairs={{0,128},{32,160},{64,192},{96,224},{128,0},{160,32},{192,64},{224,... | collective-permute-start | bytes 200 | tf_op jit(solution)/shard_map/ppermute | solution.py:38
  269.1 10.2 %collective-permute-start.31 = (f32[16,6,320]{2,0,1:T(8,128)S(1)}, f32[16,6,320]{2,0,1:T(8,128)S(1)}, u32[]{:S(2)}, u32[]{:S(2)}) collective-permute-start(f32[16,6,320]{2,0,1:T(8,128)S(1)} %get-tuple-element.14), channel_id=1, source_target_pairs={{0,1},{1,2},{2,3},{3,4},{4,5},{5,6},{6,7},{7,8},{8,9},{9,10},{10,1... | collective-permute-start | bytes 368648 | tf_op jit(solution)/shard_map/ppermute | solution.py:21
  271.8 6.9 %collective-permute-start.30 = (f32[16]{0:T(128)S(1)}, f32[16]{0:T(128)S(1)}, u32[]{:S(2)}, u32[]{:S(2)}) collective-permute-start(f32[16]{0:T(128)S(1)} %add.254), channel_id=1, source_target_pairs={{0,256},{32,288},{64,320},{96,352},{128,384},{160,416},{192,448},{... | collective-permute-start | bytes 200 | tf_op jit(solution)/shard_map/ppermute | solution.py:38
  275.8 3.6 collective-permute-start.32
  290.1 34.7 %copy-start.8 = (f32[16,64,64]{2,1,0:T(8,128)S(1)}, f32[16,64,64]{2,1,0:T(8,128)}, u32[]{:S(2)}) copy-start(f32[16,64,64]{2,1,0:T(8,128)} %param.16) | copy-start | bytes 786436
  290.2 34.7 %copy-start.18 = (f32[16,16,64]{2,1,0:T(8,128)S(1)}, f32[16,16,64]{2,1,0:T(8,128)}, u32[]{:S(2)}) copy-start(f32[16,16,64]{2,1,0:T(8,128)} %convolution_bitcast_fusion.2) | copy-start | bytes 196612
  290.2 34.7 %copy-start.20 = (f32[16,16,64]{2,1,0:T(8,128)S(1)}, f32[16,16,64]{2,1,0:T(8,128)}, u32[]{:S(2)}) copy-start(f32[16,16,64]{2,1,0:T(8,128)} %convolution_bitcast_fusion.4) | copy-start | bytes 196612
  290.2 35.6 %copy-start.3 = (f32[16,16,256]{2,1,0:T(8,128)S(1)}, f32[16,16,256]{2,1,0:T(8,128)}, u32[]{:S(2)}) copy-start(f32[16,16,256]{2,1,0:T(8,128)} %param.11) | copy-start | bytes 786436
  290.2 35.6 %copy-start.5 = (f32[16,16,256]{2,0,1:T(8,128)S(1)}, f32[16,16,256]{2,0,1:T(8,128)}, u32[]{:S(2)}) copy-start(f32[16,16,256]{2,0,1:T(8,128)} %copy-done.4) | copy-start | bytes 786436
  290.2 35.6 %copy-start.10 = (f32[16,16,256]{2,0,1:T(8,128)S(1)}, f32[16,16,256]{2,0,1:T(8,128)}, u32[]{:S(2)}) copy-start(f32[16,16,256]{2,0,1:T(8,128)} %copy-done.9) | copy-start | bytes 786436
  326.7 3.2 collective-permute-start.33
  329.9 5.4 %collective-permute-start.34 = (f32[16]{0:T(128)S(1)}, f32[16]{0:T(128)S(1)}, u32[]{:S(2)}, u32[]{:S(2)}) collective-permute-start(f32[16]{0:T(128)S(1)} %add.262), channel_id=1, source_target_pairs={{0,2},{1,3},{2,0},{3,1},{4,6},{5,7},{6,4},{7,5},{8,10},{9,11},{10,... | collective-permute-start | bytes 200 | tf_op jit(solution)/shard_map/ppermute | solution.py:38
  335.3 6.3 %collective-permute-start.35 = (f32[16]{0:T(128)S(1)}, f32[16]{0:T(128)S(1)}, u32[]{:S(2)}, u32[]{:S(2)}) collective-permute-start(f32[16]{0:T(128)S(1)} %add.263), channel_id=1, source_target_pairs={{0,4},{1,5},{2,6},{3,7},{4,0},{5,1},{6,2},{7,3},{8,12},{9,13},{10,... | collective-permute-start | bytes 200 | tf_op jit(solution)/shard_map/ppermute | solution.py:38
  341.6 9.3 %collective-permute-start.36 = (f32[16]{0:T(128)S(1)}, f32[16]{0:T(128)S(1)}, u32[]{:S(2)}, u32[]{:S(2)}) collective-permute-start(f32[16]{0:T(128)S(1)} %add.264), channel_id=1, source_target_pairs={{0,8},{1,9},{2,10},{3,11},{4,12},{5,13},{6,14},{7,15},{8,0},{9,1},... | collective-permute-start | bytes 200 | tf_op jit(solution)/shard_map/ppermute | solution.py:38
  350.9 14.1 %collective-permute-start.37 = (f32[16]{0:T(128)S(1)}, f32[16]{0:T(128)S(1)}, u32[]{:S(2)}, u32[]{:S(2)}) collective-permute-start(f32[16]{0:T(128)S(1)} %add.265), channel_id=1, source_target_pairs={{0,16},{1,17},{2,18},{3,19},{4,20},{5,21},{6,22},{7,23},{8,24},{9,... | collective-permute-start | bytes 200 | tf_op jit(solution)/shard_map/ppermute | solution.py:38
  365.1 5.4 %collective-permute-start.38 = (f32[16]{0:T(128)S(1)}, f32[16]{0:T(128)S(1)}, u32[]{:S(2)}, u32[]{:S(2)}) collective-permute-start(f32[16]{0:T(128)S(1)} %add.266), channel_id=1, source_target_pairs={{0,32},{32,0},{64,96},{96,64},{128,160},{160,128},{192,224},{224,1... | collective-permute-start | bytes 200 | tf_op jit(solution)/shard_map/ppermute | solution.py:38
  370.5 6.9 %collective-permute-start.39 = (f32[16]{0:T(128)S(1)}, f32[16]{0:T(128)S(1)}, u32[]{:S(2)}, u32[]{:S(2)}) collective-permute-start(f32[16]{0:T(128)S(1)} %add.267), channel_id=1, source_target_pairs={{0,64},{32,96},{64,0},{96,32},{128,192},{160,224},{192,128},{224,1... | collective-permute-start | bytes 200 | tf_op jit(solution)/shard_map/ppermute | solution.py:38
  377.4 5.4 %collective-permute-start.40 = (f32[16]{0:T(128)S(1)}, f32[16]{0:T(128)S(1)}, u32[]{:S(2)}, u32[]{:S(2)}) collective-permute-start(f32[16]{0:T(128)S(1)} %add.268), channel_id=1, source_target_pairs={{0,128},{32,160},{64,192},{96,224},{128,0},{160,32},{192,64},{224,... | collective-permute-start | bytes 200 | tf_op jit(solution)/shard_map/ppermute | solution.py:38
  382.9 6.9 %collective-permute-start.41 = (f32[16]{0:T(128)S(1)}, f32[16]{0:T(128)S(1)}, u32[]{:S(2)}, u32[]{:S(2)}) collective-permute-start(f32[16]{0:T(128)S(1)} %add.269), channel_id=1, source_target_pairs={{0,256},{32,288},{64,320},{96,352},{128,384},{160,416},{192,448},{... | collective-permute-start | bytes 200 | tf_op jit(solution)/shard_map/ppermute | solution.py:38
  (22 other events, 67.7 us)
where the time goes:
time: 394 us; the launch traced here: 392 us
  starting transfers between devices  140 us (36%)
  waiting for transfers between devices  85.8 us (22%)
  matrix products  85 us (22%)
  blocking collectives  44.7 us (11%)
  local copies, waits for them, and re-layouts  20.7 us (5%)
  other arithmetic  13.6 us (3%)
    ppermute x36, starting transfers between devices, all_sum(): lax.ppermute(vector, axis, [(i, i ^ stride) for i in range(count)])  133 us
    ppermute x36, waiting for transfers between devices, all_sum(): lax.ppermute(vector, axis, [(i, i ^ stride) for i in range(count)])  85.8 us
    dot_general x2, matrix products, covariance_apply(): jnp.einsum('lspq,mlsq->mlp', near_blocks, rim_values[:, near_rows], preci...  66.9 us
    all_gather x2, blocking collectives, covariance_apply(): band_coeffs = lax.all_gather(panel_coeffs, 'band', axis=1, tiled=True)  44.7 us
  transfers between devices with their start and end apart: 42, of which 26 were waited for; matrix products, arithmetic and copies ran while one was open for 17% of the time, Pallas kernels for 0%

commit v1 on v0

--- a/solution.py
+++ b/solution.py
@@ -113,7 +113,9 @@
         )
         upward = jnp.einsum("lab,mla->mlb", transfer, coeffs, precision=HIGHEST_PRECISION)
         panel_coeffs = jnp.einsum("lk,mlb->mkb", membership, upward, precision=HIGHEST_PRECISION)
-        band_coeffs = lax.all_gather(panel_coeffs, "band", axis=1, tiled=True)
+        band_coeffs = jnp.concatenate(
+            lax.all_to_all(jnp.stack([panel_coeffs] * lax.axis_size("band")), "band", 0, 0), axis=1
+        )
         panel_far = jnp.einsum(
             "ksab,mksb->mka",
             panel_couple,

time: 394 us -> 376 us (0.954)
  the two profiles are of different devices: /device:TPU:32 before, /device:TPU:2 now
where the time goes in v1:
time: 376 us; the launch traced here: 374 us
  starting transfers between devices  149 us (40%)
  waiting for transfers between devices  91 us (24%)
  matrix products  86.2 us (23%)
  local copies, waits for them, and re-layouts  25.8 us (7%)
  other arithmetic  20.1 us (5%)
    ppermute x36, starting transfers between devices, all_sum(): lax.ppermute(vector, axis, [(i, i ^ stride) for i in range(count)])  123 us
    ppermute x36, waiting for transfers between devices, all_sum(): lax.ppermute(vector, axis, [(i, i ^ stride) for i in range(count)])  91 us
    dot_general x2, matrix products, covariance_apply(): jnp.einsum('lspq,mlsq->mlp', near_blocks, rim_values[:, near_rows], preci...  66.7 us
    all_to_all x2, starting transfers between devices, covariance_apply(): lax.all_to_all(jnp.stack([panel_coeffs] * lax.axis_size('band')), 'band',...  12.9 us
    ppermute x3, starting transfers between devices, extended(): lax.ppermute(head, axis, [((i + 1) % count, i) for i in range(count)])  12.1 us
    unnamed x96, local copies, waits for them, and re-layouts  8.14 us
  transfers between devices with their start and end apart: 44, of which 26 were waited for; matrix products, arithmetic and copies ran while one was open for 20% of the time, Pallas kernels for 0%

profile of v1, /device:TPU:2, one launch (start us, length us, event | category | flops | bytes accessed | tf_op | source)
XLA Modules:
  0.0 373.7 jit_solution(9890674670201344755)
XLA Ops:
  2.5 1.9 collective-permute-start
  6.3 9.1 %collective-permute-start.12 = (f32[3,2,256]{2,0,1:T(4,128)}, f32[3,2,256]{2,0,1:T(4,128)S(1)}, u32[]{:S(2)}, u32[]{:S(2)}) collective-permute-start(f32[3,2,256]{2,0,1:T(4,128)} %get-tuple-element.22), channel_id=1, source_target_pairs={{1,0},{2,1},{3,2},{4,3},{5,4},{6,5},{7,6},{8,7},{9,8},{10,9},{11,1... | collective-permute-start | bytes 18440 | tf_op jit(solution)/shard_map/ppermute | solution.py:23
  15.5 2.4 convolution_bitcast_fusion.7
  19.5 7.5 %all-to-all-start = ((f32[16,1,2048]{2,1,0:T(1,128)}), f32[16,1,2048]{2,1,0:T(1,128)}, u32[]{:S(2)}, u32[]{:S(2)}) async-start(f32[16,1,2048]{2,1,0:T(1,128)} %reshape.113), calls=%async_computation | async-start | bytes 262144 | tf_op jit(solution)/shard_map/all_to_all | solution.py:117
  27.9 3.0 collective-permute-start.10
  35.8 3.4 collective-permute-done.1
  41.7 3.8 %collective-permute-done.2 = f32[16]{0:T(128)S(1)} collective-permute-done((f32[16]{0:T(128)S(1)}, f32[16]{0:T(128)S(1)}, u32[]{:S(2)}, u32[]{:S(2)}) %collective-permute-start.2) | collective-permute-done | bytes 96 | tf_op jit(solution)/shard_map/ppermute | solution.py:38
  45.5 2.4 collective-permute-start.3
  48.6 6.2 %collective-permute-done.3 = f32[16]{0:T(128)S(1)} collective-permute-done((f32[16]{0:T(128)S(1)}, f32[16]{0:T(128)S(1)}, u32[]{:S(2)}, u32[]{:S(2)}) %collective-permute-start.3) | collective-permute-done | bytes 96 | tf_op jit(solution)/shard_map/ppermute | solution.py:38
  55.5 9.1 %collective-permute-start.4 = (f32[16]{0:T(128)}, f32[16]{0:T(128)}, u32[]{:S(2)}, u32[]{:S(2)}) collective-permute-start(f32[16]{0:T(128)} %add.211), channel_id=1, source_target_pairs={{0,16},{1,17},{2,18},{3,19},{4,20},{5,21},{6,22},{7,23},{8,24},{9,... | collective-permute-start | bytes 200 | tf_op jit(solution)/shard_map/ppermute | solution.py:38
  76.9 3.0 convolution_bitcast_fusion.5
  80.9 32.3 %fusion.27 = f32[16,16,256]{2,0,1:T(8,128)S(1)} fusion(f32[16,16,5,256]{3,0,2,1:T(8,128)S(1)} %bitcast.143, f32[16,5]{1,0:T(8,128)S(1)} %copy-done.34, f32[16,5,256]{2,1,0:T(8,128)S(1)} %copy-done.22, f32[16,256]{1,0:T(8,128)S(1)} %copy-done.28, f32[16,5,256]{2,1,0:T(8,128)S(1)} %copy-done.21, f32[16,256]{1,0:T(8,128)S(1)} %copy-done.30, ...), kind=kOutput, calls=%fused_computation.39 | convolution fusion | flops 1080164352 | bytes 2146624 | tf_op jit(solution)/shard_map/lspq,mlsq->mlp/dot_general | solution.py:108
  114.0 1.9 collective-permute-start.13
  117.1 1.9 collective-permute-start.14
  119.0 3.4 collective-permute-start.5
  124.4 4.4 %collective-permute-done.15 = f32[16]{0:T(128)S(1)} collective-permute-done((f32[16]{0:T(128)S(1)}, f32[16]{0:T(128)S(1)}, u32[]{:S(2)}, u32[]{:S(2)}) %collective-permute-start.15) | collective-permute-done | bytes 96 | tf_op jit(solution)/shard_map/ppermute | solution.py:38
  128.8 4.3 %collective-permute-start.16 = (f32[16]{0:T(128)S(1)}, f32[16]{0:T(128)S(1)}, u32[]{:S(2)}, u32[]{:S(2)}) collective-permute-start(f32[16]{0:T(128)S(1)} %add.240), channel_id=1, source_target_pairs={{0,8},{1,9},{2,10},{3,11},{4,12},{5,13},{6,14},{7,15},{8,0},{9,1},... | collective-permute-start | bytes 200 | tf_op jit(solution)/shard_map/ppermute | solution.py:38
  133.1 4.9 %collective-permute-start.6 = (f32[16]{0:T(128)S(1)}, f32[16]{0:T(128)S(1)}, u32[]{:S(2)}, u32[]{:S(2)}) collective-permute-start(f32[16]{0:T(128)S(1)} %add.213), channel_id=1, source_target_pairs={{0,64},{32,96},{64,0},{96,32},{128,192},{160,224},{192,128},{224,1... | collective-permute-start | bytes 200 | tf_op jit(solution)/shard_map/ppermute | solution.py:38
  138.1 5.5 %collective-permute-start.17 = (f32[16]{0:T(128)S(1)}, f32[16]{0:T(128)S(1)}, u32[]{:S(2)}, u32[]{:S(2)}) collective-permute-start(f32[16]{0:T(128)S(1)} %add.241), channel_id=1, source_target_pairs={{0,16},{1,17},{2,18},{3,19},{4,20},{5,21},{6,22},{7,23},{8,24},{9,... | collective-permute-start | bytes 200 | tf_op jit(solution)/shard_map/ppermute | solution.py:38
  143.7 8.6 %collective-permute-done.17 = f32[16]{0:T(128)S(1)} collective-permute-done((f32[16]{0:T(128)S(1)}, f32[16]{0:T(128)S(1)}, u32[]{:S(2)}, u32[]{:S(2)}) %collective-permute-start.17) | collective-permute-done | bytes 96 | tf_op jit(solution)/shard_map/ppermute | solution.py:38
  152.3 3.4 collective-permute-start.18
  155.7 2.5 collective-permute-start.7
  158.2 4.6 %collective-permute-start.19 = (f32[16]{0:T(128)S(1)}, f32[16]{0:T(128)S(1)}, u32[]{:S(2)}, u32[]{:S(2)}) collective-permute-start(f32[16]{0:T(128)S(1)} %add.243), channel_id=1, source_target_pairs={{0,64},{32,96},{64,0},{96,32},{128,192},{160,224},{192,128},{224,1... | collective-permute-start | bytes 200 | tf_op jit(solution)/shard_map/ppermute | solution.py:38
  162.8 2.3 collective-permute-done.19
  165.1 3.4 collective-permute-start.20
  168.5 4.0 %collective-permute-start.8 = (f32[16]{0:T(128)S(1)}, f32[16]{0:T(128)S(1)}, u32[]{:S(2)}, u32[]{:S(2)}) collective-permute-start(f32[16]{0:T(128)S(1)} %add.215), channel_id=1, source_target_pairs={{0,256},{32,288},{64,320},{96,352},{128,384},{160,416},{192,448},{... | collective-permute-start | bytes 200 | tf_op jit(solution)/shard_map/ppermute | solution.py:38
  172.5 3.4 collective-permute-start.21
  175.9 3.6 collective-permute-done.21
  180.2 2.1 collective-permute-start.22
  183.9 2.9 collective-permute-start.23
  187.0 2.3 collective-permute-done.23
  191.2 4.4 %collective-permute-done.24 = f32[16]{0:T(128)S(1)} collective-permute-done((f32[16]{0:T(128)S(1)}, f32[16]{0:T(128)S(1)}, u32[]{:S(2)}, u32[]{:S(2)}) %collective-permute-start.24) | collective-permute-done | bytes 96 | tf_op jit(solution)/shard_map/ppermute | solution.py:38
  195.6 4.4 %collective-permute-start.25 = (f32[16]{0:T(128)S(1)}, f32[16]{0:T(128)S(1)}, u32[]{:S(2)}, u32[]{:S(2)}) collective-permute-start(f32[16]{0:T(128)S(1)} %add.249), channel_id=1, source_target_pairs={{0,8},{1,9},{2,10},{3,11},{4,12},{5,13},{6,14},{7,15},{8,0},{9,1},... | collective-permute-start | bytes 200 | tf_op jit(solution)/shard_map/ppermute | solution.py:38
  200.8 4.2 %collective-permute-done.25 = f32[16]{0:T(128)S(1)} collective-permute-done((f32[16]{0:T(128)S(1)}, f32[16]{0:T(128)S(1)}, u32[]{:S(2)}, u32[]{:S(2)}) %collective-permute-start.25) | collective-permute-done | bytes 96 | tf_op jit(solution)/shard_map/ppermute | solution.py:38
  205.0 5.5 %collective-permute-start.26 = (f32[16]{0:T(128)S(1)}, f32[16]{0:T(128)S(1)}, u32[]{:S(2)}, u32[]{:S(2)}) collective-permute-start(f32[16]{0:T(128)S(1)} %add.250), channel_id=1, source_target_pairs={{0,16},{1,17},{2,18},{3,19},{4,20},{5,21},{6,22},{7,23},{8,24},{9,... | collective-permute-start | bytes 200 | tf_op jit(solution)/shard_map/ppermute | solution.py:38
  211.2 7.9 %collective-permute-done.26 = f32[16]{0:T(128)S(1)} collective-permute-done((f32[16]{0:T(128)S(1)}, f32[16]{0:T(128)S(1)}, u32[]{:S(2)}, u32[]{:S(2)}) %collective-permute-start.26) | collective-permute-done | bytes 96 | tf_op jit(solution)/shard_map/ppermute | solution.py:38
  219.6 2.5 collective-permute-start.27
  226.5 4.6 %collective-permute-start.28 = (f32[16]{0:T(128)}, f32[16]{0:T(128)}, u32[]{:S(2)}, u32[]{:S(2)}) collective-permute-start(f32[16]{0:T(128)} %add.252), channel_id=1, source_target_pairs={{0,64},{32,96},{64,0},{96,32},{128,192},{160,224},{192,128},{224,1... | collective-permute-start | bytes 200 | tf_op jit(solution)/shard_map/ppermute | solution.py:38
  231.1 5.4 %all-to-all-start.1 = ((f32[16,1,2048]{2,1,0:T(1,128)}), f32[16,1,2048]{2,1,0:T(1,128)}, u32[]{:S(2)}, u32[]{:S(2)}) async-start(f32[16,1,2048]{2,1,0:T(1,128)} %reshape.115), calls=%async_computation.1 | async-start | bytes 262144 | tf_op jit(solution)/shard_map/all_to_all | solution.py:117
  237.1 2.2 collective-permute-start.29
  239.3 3.2 collective-permute-done.29
  242.5 4.0 %collective-permute-start.30 = (f32[16]{0:T(128)S(1)}, f32[16]{0:T(128)S(1)}, u32[]{:S(2)}, u32[]{:S(2)}) collective-permute-start(f32[16]{0:T(128)S(1)} %add.254), channel_id=1, source_target_pairs={{0,256},{32,288},{64,320},{96,352},{128,384},{160,416},{192,448},{... | collective-permute-start | bytes 200 | tf_op jit(solution)/shard_map/ppermute | solution.py:38
  246.6 2.9 collective-permute-done.30
  250.5 2.5 reduce.1
  254.8 2.2 gather_fusion.6
  260.3 2.4 gather_fusion.5
  262.7 3.5 convolution_bitcast_fusion.4
  272.4 34.5 %fusion.26 = f32[16,16,256]{2,0,1:T(8,128)S(1)} fusion(f32[16,16,5,256]{3,0,2,1:T(8,128)} %bitcast.144, f32[16,5]{1,0:T(8,128)S(1)} %copy-done.34, f32[16,5,256]{2,1,0:T(8,128)} %get-tuple-element.16, f32[16,256]{1,0:T(8,128)S(1)} %copy-done.29, f32[16,5,256]{2,1,0:T(8,128)} %get-tuple-element.15, f32[16,256]{1,0:T(8,128)S(1)} %copy-done.31, ...), kind=kOutput, calls=%fused_computation.38 | convolution fusion | flops 1080164352 | bytes 2146624 | tf_op jit(solution)/shard_map/lspq,mlsq->mlp/dot_general | solution.py:108
  308.7 1.9 collective-permute-start.33
  311.8 3.2 collective-permute-start.34
  315.0 2.2 collective-permute-done.34
  319.1 4.4 %collective-permute-done.35 = f32[16]{0:T(128)S(1)} collective-permute-done((f32[16]{0:T(128)S(1)}, f32[16]{0:T(128)S(1)}, u32[]{:S(2)}, u32[]{:S(2)}) %collective-permute-start.35) | collective-permute-done | bytes 96 | tf_op jit(solution)/shard_map/ppermute | solution.py:38
  323.5 4.3 %collective-permute-start.36 = (f32[16]{0:T(128)S(1)}, f32[16]{0:T(128)S(1)}, u32[]{:S(2)}, u32[]{:S(2)}) collective-permute-start(f32[16]{0:T(128)S(1)} %add.264), channel_id=1, source_target_pairs={{0,8},{1,9},{2,10},{3,11},{4,12},{5,13},{6,14},{7,15},{8,0},{9,1},... | collective-permute-start | bytes 200 | tf_op jit(solution)/shard_map/ppermute | solution.py:38
  327.8 5.0 %collective-permute-done.36 = f32[16]{0:T(128)S(1)} collective-permute-done((f32[16]{0:T(128)S(1)}, f32[16]{0:T(128)S(1)}, u32[]{:S(2)}, u32[]{:S(2)}) %collective-permute-start.36) | collective-permute-done | bytes 96 | tf_op jit(solution)/shard_map/ppermute | solution.py:38
  332.8 5.5 %collective-permute-start.37 = (f32[16]{0:T(128)S(1)}, f32[16]{0:T(128)S(1)}, u32[]{:S(2)}, u32[]{:S(2)}) collective-permute-start(f32[16]{0:T(128)S(1)} %add.265), channel_id=1, source_target_pairs={{0,16},{1,17},{2,18},{3,19},{4,20},{5,21},{6,22},{7,23},{8,24},{9,... | collective-permute-start | bytes 200 | tf_op jit(solution)/shard_map/ppermute | solution.py:38
  338.3 8.6 %collective-permute-done.37 = f32[16]{0:T(128)S(1)} collective-permute-done((f32[16]{0:T(128)S(1)}, f32[16]{0:T(128)S(1)}, u32[]{:S(2)}, u32[]{:S(2)}) %collective-permute-start.37) | collective-permute-done | bytes 96 | tf_op jit(solution)/shard_map/ppermute | solution.py:38
  347.0 3.4 collective-permute-start.38
  350.4 2.0 collective-permute-done.38
  352.4 4.9 %collective-permute-start.39 = (f32[16]{0:T(128)S(1)}, f32[16]{0:T(128)S(1)}, u32[]{:S(2)}, u32[]{:S(2)}) collective-permute-start(f32[16]{0:T(128)S(1)} %add.267), channel_id=1, source_target_pairs={{0,64},{32,96},{64,0},{96,32},{128,192},{160,224},{192,128},{224,1... | collective-permute-start | bytes 200 | tf_op jit(solution)/shard_map/ppermute | solution.py:38
  357.3 2.0 collective-permute-done.39
  359.3 2.2 collective-permute-start.40
  361.5 3.3 collective-permute-done.40
  364.8 4.0 %collective-permute-start.41 = (f32[16]{0:T(128)S(1)}, f32[16]{0:T(128)S(1)}, u32[]{:S(2)}, u32[]{:S(2)}) collective-permute-start(f32[16]{0:T(128)S(1)} %add.269), channel_id=1, source_target_pairs={{0,256},{32,288},{64,320},{96,352},{128,384},{160,416},{192,448},{... | collective-permute-start | bytes 200 | tf_op jit(solution)/shard_map/ppermute | solution.py:38
  368.8 2.9 collective-permute-done.41
  (215 shorter events, 62.8 us)
Async XLA Ops:
  0.6 76.3 %copy-start = (f32[16,4,64,64]{3,2,1,0:T(8,128)S(1)}, f32[16,4,64,64]{3,2,1,0:T(8,128)}, u32[]{:S(2)}) copy-start(f32[16,4,64,64]{3,2,1,0:T(8,128)} %param.15) | copy-start | bytes 3145732
  0.6 26.3 %copy-start.2 = (f32[16,16,256]{2,1,0:T(8,128)S(1)}, f32[16,16,256]{2,1,0:T(8,128)}, u32[]{:S(2)}) copy-start(f32[16,16,256]{2,1,0:T(8,128)} %param.11) | copy-start | bytes 786436
  2.5 30.6 %collective-permute-start = (f32[16]{0:T(128)}, f32[16]{0:T(128)}, u32[]{:S(2)}, u32[]{:S(2)}) collective-permute-start(f32[16]{0:T(128)} %multiply_reduce_fusion.3), channel_id=1, source_target_pairs={{0,1},{1,0},{2,3},{3,2},{4,5},{5,4},{6,7},{7,6},{8,9},{9,8},{10,11... | collective-permute-start | bytes 200 | tf_op jit(solution)/shard_map/ppermute | solution.py:38
  5.8 58.7 %collective-permute-start.11 = (f32[3,2,256]{2,0,1:T(4,128)}, f32[3,2,256]{2,0,1:T(4,128)S(1)}, u32[]{:S(2)}, u32[]{:S(2)}) collective-permute-start(f32[3,2,256]{2,0,1:T(4,128)} %get-tuple-element.21), channel_id=1, source_target_pairs={{0,1},{1,2},{2,3},{3,4},{4,5},{5,6},{6,7},{7,8},{8,9},{9,10},{10,1... | collective-permute-start | bytes 18440 | tf_op jit(solution)/shard_map/ppermute | solution.py:21
  6.3 24.6 %copy-start.38 = (s32[16,4]{0,1:T(4,128)S(1)}, s32[16,4]{0,1:T(4,128)}, u32[]{:S(2)}) copy-start(s32[16,4]{0,1:T(4,128)} %param.19) | copy-start | bytes 772
  6.3 26.1 %copy-start.19 = (f32[3,16,256]{2,1,0:T(8,128)S(1)}, f32[3,16,256]{2,1,0:T(8,128)}, u32[]{:S(2)}) copy-start(f32[3,16,256]{2,1,0:T(8,128)} %param.13) | copy-start | bytes 147460
  6.3 58.2 %collective-permute-start.12 = (f32[3,2,256]{2,0,1:T(4,128)}, f32[3,2,256]{2,0,1:T(4,128)S(1)}, u32[]{:S(2)}, u32[]{:S(2)}) collective-permute-start(f32[3,2,256]{2,0,1:T(4,128)} %get-tuple-element.22), channel_id=1, source_target_pairs={{1,0},{2,1},{3,2},{4,3},{5,4},{6,5},{7,6},{8,7},{9,8},{10,9},{11,1... | collective-permute-start | bytes 18440 | tf_op jit(solution)/shard_map/ppermute | solution.py:23
  19.5 46.8 %all-to-all-start = ((f32[16,1,2048]{2,1,0:T(1,128)}), f32[16,1,2048]{2,1,0:T(1,128)}, u32[]{:S(2)}, u32[]{:S(2)}) async-start(f32[16,1,2048]{2,1,0:T(1,128)} %reshape.113), calls=%async_computation | async-start | bytes 262144 | tf_op jit(solution)/shard_map/all_to_all | solution.py:117
  27.1 42.3 %copy-start.16 = (f32[2,2,64,64]{3,2,1,0:T(8,128)S(1)}, f32[2,2,64,64]{3,2,1,0:T(8,128)}, u32[]{:S(2)}) copy-start(f32[2,2,64,64]{3,2,1,0:T(8,128)} %param.17) | copy-start | bytes 196612
  27.9 43.9 %collective-permute-start.9 = (f32[16,6,320]{2,0,1:T(8,128)}, f32[16,6,320]{2,0,1:T(8,128)}, u32[]{:S(2)}, u32[]{:S(2)}) collective-permute-start(f32[16,6,320]{2,0,1:T(8,128)} %get-tuple-element.17), channel_id=1, source_target_pairs={{0,1},{1,2},{2,3},{3,4},{4,5},{5,6},{6,7},{7,8},{8,9},{9,10},{10,1... | collective-permute-start | bytes 368648 | tf_op jit(solution)/shard_map/ppermute | solution.py:21
  27.9 43.9 %collective-permute-start.10 = (f32[16,6,320]{2,0,1:T(8,128)}, f32[16,6,320]{2,0,1:T(8,128)}, u32[]{:S(2)}, u32[]{:S(2)}) collective-permute-start(f32[16,6,320]{2,0,1:T(8,128)} %get-tuple-element.18), channel_id=1, source_target_pairs={{1,0},{2,1},{3,2},{4,3},{5,4},{6,5},{7,6},{8,7},{9,8},{10,9},{11,1... | collective-permute-start | bytes 368648 | tf_op jit(solution)/shard_map/ppermute | solution.py:23
  33.8 5.4 %collective-permute-start.1 = (f32[16]{0:T(128)S(1)}, f32[16]{0:T(128)S(1)}, u32[]{:S(2)}, u32[]{:S(2)}) collective-permute-start(f32[16]{0:T(128)S(1)} %add.208), channel_id=1, source_target_pairs={{0,2},{1,3},{2,0},{3,1},{4,6},{5,7},{6,4},{7,5},{8,10},{9,11},{10,... | collective-permute-start | bytes 200 | tf_op jit(solution)/shard_map/ppermute | solution.py:38
  39.2 6.3 %collective-permute-start.2 = (f32[16]{0:T(128)S(1)}, f32[16]{0:T(128)S(1)}, u32[]{:S(2)}, u32[]{:S(2)}) collective-permute-start(f32[16]{0:T(128)S(1)} %add.209), channel_id=1, source_target_pairs={{0,4},{1,5},{2,6},{3,7},{4,0},{5,1},{6,2},{7,3},{8,12},{9,13},{10,... | collective-permute-start | bytes 200 | tf_op jit(solution)/shard_map/ppermute | solution.py:38
  45.5 9.3 %collective-permute-start.3 = (f32[16]{0:T(128)S(1)}, f32[16]{0:T(128)S(1)}, u32[]{:S(2)}, u32[]{:S(2)}) collective-permute-start(f32[16]{0:T(128)S(1)} %add.210), channel_id=1, source_target_pairs={{0,8},{1,9},{2,10},{3,11},{4,12},{5,13},{6,14},{7,15},{8,0},{9,1},... | collective-permute-start | bytes 200 | tf_op jit(solution)/shard_map/ppermute | solution.py:38
  55.5 60.5 %collective-permute-start.4 = (f32[16]{0:T(128)}, f32[16]{0:T(128)}, u32[]{:S(2)}, u32[]{:S(2)}) collective-permute-start(f32[16]{0:T(128)} %add.211), channel_id=1, source_target_pairs={{0,16},{1,17},{2,18},{3,19},{4,20},{5,21},{6,22},{7,23},{8,24},{9,... | collective-permute-start | bytes 200 | tf_op jit(solution)/shard_map/ppermute | solution.py:38
  80.9 32.3 %copy-start.1 = (f32[16,256,64]{1,2,0:T(8,128)S(1)}, f32[16,256,64]{1,2,0:T(8,128)}, u32[]{:S(2)}) copy-start(f32[16,256,64]{1,2,0:T(8,128)} %param.14) | copy-start | bytes 3145732
  113.2 70.1 %copy-start.8 = (f32[16,64,64]{2,1,0:T(8,128)S(1)}, f32[16,64,64]{2,1,0:T(8,128)}, u32[]{:S(2)}) copy-start(f32[16,64,64]{2,1,0:T(8,128)} %param.16) | copy-start | bytes 786436
  113.2 73.6 %copy-start.33 = (s32[16]{0:T(128)S(1)}, s32[16]{0:T(128)}, u32[]{:S(2)}) copy-start(s32[16]{0:T(128)} %param.21) | copy-start | bytes 196
  114.0 97.1 %copy-start.10 = (f32[16,16,256]{2,0,1:T(8,128)}, f32[16,16,256]{2,0,1:T(8,128)S(1)}, u32[]{:S(2)}) copy-start(f32[16,16,256]{2,0,1:T(8,128)S(1)} %get-tuple-element.27) | copy-start | bytes 786436
  114.0 3.0 collective-permute-start.13
  117.1 5.4 %collective-permute-start.14 = (f32[16]{0:T(128)S(1)}, f32[16]{0:T(128)S(1)}, u32[]{:S(2)}, u32[]{:S(2)}) collective-permute-start(f32[16]{0:T(128)S(1)} %add.238), channel_id=1, source_target_pairs={{0,2},{1,3},{2,0},{3,1},{4,6},{5,7},{6,4},{7,5},{8,10},{9,11},{10,... | collective-permute-start | bytes 200 | tf_op jit(solution)/shard_map/ppermute | solution.py:38
  119.0 5.4 %collective-permute-start.5 = (f32[16]{0:T(128)S(1)}, f32[16]{0:T(128)S(1)}, u32[]{:S(2)}, u32[]{:S(2)}) collective-permute-start(f32[16]{0:T(128)S(1)} %add.212), channel_id=1, source_target_pairs={{0,32},{32,0},{64,96},{96,64},{128,160},{160,128},{192,224},{224,1... | collective-permute-start | bytes 200 | tf_op jit(solution)/shard_map/ppermute | solution.py:38
  122.5 6.3 %collective-permute-start.15 = (f32[16]{0:T(128)S(1)}, f32[16]{0:T(128)S(1)}, u32[]{:S(2)}, u32[]{:S(2)}) collective-permute-start(f32[16]{0:T(128)S(1)} %add.239), channel_id=1, source_target_pairs={{0,4},{1,5},{2,6},{3,7},{4,0},{5,1},{6,2},{7,3},{8,12},{9,13},{10,... | collective-permute-start | bytes 200 | tf_op jit(solution)/shard_map/ppermute | solution.py:38
  128.8 9.3 %collective-permute-start.16 = (f32[16]{0:T(128)S(1)}, f32[16]{0:T(128)S(1)}, u32[]{:S(2)}, u32[]{:S(2)}) collective-permute-start(f32[16]{0:T(128)S(1)} %add.240), channel_id=1, source_target_pairs={{0,8},{1,9},{2,10},{3,11},{4,12},{5,13},{6,14},{7,15},{8,0},{9,1},... | collective-permute-start | bytes 200 | tf_op jit(solution)/shard_map/ppermute | solution.py:38
  133.1 10.5 %collective-permute-start.6 = (f32[16]{0:T(128)S(1)}, f32[16]{0:T(128)S(1)}, u32[]{:S(2)}, u32[]{:S(2)}) collective-permute-start(f32[16]{0:T(128)S(1)} %add.213), channel_id=1, source_target_pairs={{0,64},{32,96},{64,0},{96,32},{128,192},{160,224},{192,128},{224,1... | collective-permute-start | bytes 200 | tf_op jit(solution)/shard_map/ppermute | solution.py:38
  138.1 14.1 %collective-permute-start.17 = (f32[16]{0:T(128)S(1)}, f32[16]{0:T(128)S(1)}, u32[]{:S(2)}, u32[]{:S(2)}) collective-permute-start(f32[16]{0:T(128)S(1)} %add.241), channel_id=1, source_target_pairs={{0,16},{1,17},{2,18},{3,19},{4,20},{5,21},{6,22},{7,23},{8,24},{9,... | collective-permute-start | bytes 200 | tf_op jit(solution)/shard_map/ppermute | solution.py:38
  152.3 5.9 %collective-permute-start.18 = (f32[16]{0:T(128)S(1)}, f32[16]{0:T(128)S(1)}, u32[]{:S(2)}, u32[]{:S(2)}) collective-permute-start(f32[16]{0:T(128)S(1)} %add.242), channel_id=1, source_target_pairs={{0,32},{32,0},{64,96},{96,64},{128,160},{160,128},{192,224},{224,1... | collective-permute-start | bytes 200 | tf_op jit(solution)/shard_map/ppermute | solution.py:38
  155.7 7.1 %collective-permute-start.7 = (f32[16]{0:T(128)S(1)}, f32[16]{0:T(128)S(1)}, u32[]{:S(2)}, u32[]{:S(2)}) collective-permute-start(f32[16]{0:T(128)S(1)} %add.214), channel_id=1, source_target_pairs={{0,128},{32,160},{64,192},{96,224},{128,0},{160,32},{192,64},{224,... | collective-permute-start | bytes 200 | tf_op jit(solution)/shard_map/ppermute | solution.py:38
  158.2 6.9 %collective-permute-start.19 = (f32[16]{0:T(128)S(1)}, f32[16]{0:T(128)S(1)}, u32[]{:S(2)}, u32[]{:S(2)}) collective-permute-start(f32[16]{0:T(128)S(1)} %add.243), channel_id=1, source_target_pairs={{0,64},{32,96},{64,0},{96,32},{128,192},{160,224},{192,128},{224,1... | collective-permute-start | bytes 200 | tf_op jit(solution)/shard_map/ppermute | solution.py:38
  165.1 7.4 %collective-permute-start.20 = (f32[16]{0:T(128)S(1)}, f32[16]{0:T(128)S(1)}, u32[]{:S(2)}, u32[]{:S(2)}) collective-permute-start(f32[16]{0:T(128)S(1)} %add.244), channel_id=1, source_target_pairs={{0,128},{32,160},{64,192},{96,224},{128,0},{160,32},{192,64},{224,... | collective-permute-start | bytes 200 | tf_op jit(solution)/shard_map/ppermute | solution.py:38
  168.5 7.4 %collective-permute-start.8 = (f32[16]{0:T(128)S(1)}, f32[16]{0:T(128)S(1)}, u32[]{:S(2)}, u32[]{:S(2)}) collective-permute-start(f32[16]{0:T(128)S(1)} %add.215), channel_id=1, source_target_pairs={{0,256},{32,288},{64,320},{96,352},{128,384},{160,416},{192,448},{... | collective-permute-start | bytes 200 | tf_op jit(solution)/shard_map/ppermute | solution.py:38
  172.5 6.9 %collective-permute-start.21 = (f32[16]{0:T(128)S(1)}, f32[16]{0:T(128)S(1)}, u32[]{:S(2)}, u32[]{:S(2)}) collective-permute-start(f32[16]{0:T(128)S(1)} %add.245), channel_id=1, source_target_pairs={{0,256},{32,288},{64,320},{96,352},{128,384},{160,416},{192,448},{... | collective-permute-start | bytes 200 | tf_op jit(solution)/shard_map/ppermute | solution.py:38
  180.2 78.6 %copy-start.5 = (f32[16,16,256]{2,0,1:T(8,128)}, f32[16,16,256]{2,0,1:T(8,128)S(1)}, u32[]{:S(2)}) copy-start(f32[16,16,256]{2,0,1:T(8,128)S(1)} %get-tuple-element.9) | copy-start | bytes 786436
  180.2 3.6 collective-permute-start.22
  183.3 77.0 %copy-start.13 = (f32[16,16,64]{2,0,1:T(8,128)}, f32[16,16,64]{2,0,1:T(8,128)S(1)}, u32[]{:S(2)}) copy-start(f32[16,16,64]{2,0,1:T(8,128)S(1)} %convolution_bitcast_fusion.6) | copy-start | bytes 196612
  183.9 5.4 %collective-permute-start.23 = (f32[16]{0:T(128)S(1)}, f32[16]{0:T(128)S(1)}, u32[]{:S(2)}, u32[]{:S(2)}) collective-permute-start(f32[16]{0:T(128)S(1)} %add.247), channel_id=1, source_target_pairs={{0,2},{1,3},{2,0},{3,1},{4,6},{5,7},{6,4},{7,5},{8,10},{9,11},{10,... | collective-permute-start | bytes 200 | tf_op jit(solution)/shard_map/ppermute | solution.py:38
  189.3 6.3 %collective-permute-start.24 = (f32[16]{0:T(128)S(1)}, f32[16]{0:T(128)S(1)}, u32[]{:S(2)}, u32[]{:S(2)}) collective-permute-start(f32[16]{0:T(128)S(1)} %add.248), channel_id=1, source_target_pairs={{0,4},{1,5},{2,6},{3,7},{4,0},{5,1},{6,2},{7,3},{8,12},{9,13},{10,... | collective-permute-start | bytes 200 | tf_op jit(solution)/shard_map/ppermute | solution.py:38
  195.6 9.3 %collective-permute-start.25 = (f32[16]{0:T(128)S(1)}, f32[16]{0:T(128)S(1)}, u32[]{:S(2)}, u32[]{:S(2)}) collective-permute-start(f32[16]{0:T(128)S(1)} %add.249), channel_id=1, source_target_pairs={{0,8},{1,9},{2,10},{3,11},{4,12},{5,13},{6,14},{7,15},{8,0},{9,1},... | collective-permute-start | bytes 200 | tf_op jit(solution)/shard_map/ppermute | solution.py:38
  205.0 14.1 %collective-permute-start.26 = (f32[16]{0:T(128)S(1)}, f32[16]{0:T(128)S(1)}, u32[]{:S(2)}, u32[]{:S(2)}) collective-permute-start(f32[16]{0:T(128)S(1)} %add.250), channel_id=1, source_target_pairs={{0,16},{1,17},{2,18},{3,19},{4,20},{5,21},{6,22},{7,23},{8,24},{9,... | collective-permute-start | bytes 200 | tf_op jit(solution)/shard_map/ppermute | solution.py:38
  219.6 5.7 %collective-permute-start.27 = (f32[16]{0:T(128)}, f32[16]{0:T(128)}, u32[]{:S(2)}, u32[]{:S(2)}) collective-permute-start(f32[16]{0:T(128)} %add.251), channel_id=1, source_target_pairs={{0,32},{32,0},{64,96},{96,64},{128,160},{160,128},{192,224},{224,1... | collective-permute-start | bytes 200 | tf_op jit(solution)/shard_map/ppermute | solution.py:38
  226.5 10.0 %collective-permute-start.28 = (f32[16]{0:T(128)}, f32[16]{0:T(128)}, u32[]{:S(2)}, u32[]{:S(2)}) collective-permute-start(f32[16]{0:T(128)} %add.252), channel_id=1, source_target_pairs={{0,64},{32,96},{64,0},{96,32},{128,192},{160,224},{192,128},{224,1... | collective-permute-start | bytes 200 | tf_op jit(solution)/shard_map/ppermute | solution.py:38
  231.1 19.5 %all-to-all-start.1 = ((f32[16,1,2048]{2,1,0:T(1,128)}), f32[16,1,2048]{2,1,0:T(1,128)}, u32[]{:S(2)}, u32[]{:S(2)}) async-start(f32[16,1,2048]{2,1,0:T(1,128)} %reshape.115), calls=%async_computation.1 | async-start | bytes 262144 | tf_op jit(solution)/shard_map/all_to_all | solution.py:117
  237.1 5.4 %collective-permute-start.29 = (f32[16]{0:T(128)S(1)}, f32[16]{0:T(128)S(1)}, u32[]{:S(2)}, u32[]{:S(2)}) collective-permute-start(f32[16]{0:T(128)S(1)} %add.253), channel_id=1, source_target_pairs={{0,128},{32,160},{64,192},{96,224},{128,0},{160,32},{192,64},{224,... | collective-permute-start | bytes 200 | tf_op jit(solution)/shard_map/ppermute | solution.py:38
  239.2 19.5 %collective-permute-start.31 = (f32[16,6,320]{2,0,1:T(8,128)}, f32[16,6,320]{2,0,1:T(8,128)}, u32[]{:S(2)}, u32[]{:S(2)}) collective-permute-start(f32[16,6,320]{2,0,1:T(8,128)} %get-tuple-element.12), channel_id=1, source_target_pairs={{0,1},{1,2},{2,3},{3,4},{4,5},{5,6},{6,7},{7,8},{8,9},{9,10},{10,1... | collective-permute-start | bytes 368648 | tf_op jit(solution)/shard_map/ppermute | solution.py:21
  242.5 6.9 %collective-permute-start.30 = (f32[16]{0:T(128)S(1)}, f32[16]{0:T(128)S(1)}, u32[]{:S(2)}, u32[]{:S(2)}) collective-permute-start(f32[16]{0:T(128)S(1)} %add.254), channel_id=1, source_target_pairs={{0,256},{32,288},{64,320},{96,352},{128,384},{160,416},{192,448},{... | collective-permute-start | bytes 200 | tf_op jit(solution)/shard_map/ppermute | solution.py:38
  246.5 12.2 %collective-permute-start.32 = (f32[16,6,320]{2,0,1:T(8,128)}, f32[16,6,320]{2,0,1:T(8,128)}, u32[]{:S(2)}, u32[]{:S(2)}) collective-permute-start(f32[16,6,320]{2,0,1:T(8,128)} %get-tuple-element.13), channel_id=1, source_target_pairs={{1,0},{2,1},{3,2},{4,3},{5,4},{6,5},{7,6},{8,7},{9,8},{10,9},{11,1... | collective-permute-start | bytes 368648 | tf_op jit(solution)/shard_map/ppermute | solution.py:23
  272.4 34.5 %copy-start.9 = (f32[16,64,64]{2,1,0:T(8,128)S(1)}, f32[16,64,64]{2,1,0:T(8,128)}, u32[]{:S(2)}) copy-start(f32[16,64,64]{2,1,0:T(8,128)} %param.16) | copy-start | bytes 786436
  272.4 34.5 %copy-start.15 = (f32[16,16,64]{2,0,1:T(8,128)S(1)}, f32[16,16,64]{2,0,1:T(8,128)}, u32[]{:S(2)}) copy-start(f32[16,16,64]{2,0,1:T(8,128)} %copy.55) | copy-start | bytes 196612
  272.4 34.5 %copy-start.17 = (f32[16,16,64]{2,1,0:T(8,128)S(1)}, f32[16,16,64]{2,1,0:T(8,128)}, u32[]{:S(2)}) copy-start(f32[16,16,64]{2,1,0:T(8,128)} %convolution_bitcast_fusion.4) | copy-start | bytes 196612
  272.4 35.5 %copy-start.4 = (f32[16,16,256]{2,1,0:T(8,128)S(1)}, f32[16,16,256]{2,1,0:T(8,128)}, u32[]{:S(2)}) copy-start(f32[16,16,256]{2,1,0:T(8,128)} %param.11) | copy-start | bytes 786436
  272.4 35.5 %copy-start.6 = (f32[16,16,256]{2,0,1:T(8,128)S(1)}, f32[16,16,256]{2,0,1:T(8,128)}, u32[]{:S(2)}) copy-start(f32[16,16,256]{2,0,1:T(8,128)} %copy-done.5) | copy-start | bytes 786436
  272.4 35.5 %copy-start.11 = (f32[16,16,256]{2,0,1:T(8,128)S(1)}, f32[16,16,256]{2,0,1:T(8,128)}, u32[]{:S(2)}) copy-start(f32[16,16,256]{2,0,1:T(8,128)} %copy-done.10) | copy-start | bytes 786436
  272.4 35.5 %copy-start.35 = (f32[16]{0:T(128)S(1)}, f32[16]{0:T(128)}, u32[]{:S(2)}) copy-start(f32[16]{0:T(128)} %get-tuple-element.6) | copy-start | bytes 196
  306.9 64.8 %copy-start.39 = (f32[16]{0:T(128)S(1)}, f32[16]{0:T(128)}, u32[]{:S(2)}) copy-start(f32[16]{0:T(128)} %get-tuple-element.7) | copy-start | bytes 196
  306.9 64.8 %copy-start.37 = (f32[16]{0:T(128)S(1)}, f32[16]{0:T(128)}, u32[]{:S(2)}) copy-start(f32[16]{0:T(128)} %copy-done.36) | copy-start | bytes 196
  308.7 3.0 collective-permute-start.33
  311.8 5.4 %collective-permute-start.34 = (f32[16]{0:T(128)S(1)}, f32[16]{0:T(128)S(1)}, u32[]{:S(2)}, u32[]{:S(2)}) collective-permute-start(f32[16]{0:T(128)S(1)} %add.262), channel_id=1, source_target_pairs={{0,2},{1,3},{2,0},{3,1},{4,6},{5,7},{6,4},{7,5},{8,10},{9,11},{10,... | collective-permute-start | bytes 200 | tf_op jit(solution)/shard_map/ppermute | solution.py:38
  317.2 6.3 %collective-permute-start.35 = (f32[16]{0:T(128)S(1)}, f32[16]{0:T(128)S(1)}, u32[]{:S(2)}, u32[]{:S(2)}) collective-permute-start(f32[16]{0:T(128)S(1)} %add.263), channel_id=1, source_target_pairs={{0,4},{1,5},{2,6},{3,7},{4,0},{5,1},{6,2},{7,3},{8,12},{9,13},{10,... | collective-permute-start | bytes 200 | tf_op jit(solution)/shard_map/ppermute | solution.py:38
  323.5 9.3 %collective-permute-start.36 = (f32[16]{0:T(128)S(1)}, f32[16]{0:T(128)S(1)}, u32[]{:S(2)}, u32[]{:S(2)}) collective-permute-start(f32[16]{0:T(128)S(1)} %add.264), channel_id=1, source_target_pairs={{0,8},{1,9},{2,10},{3,11},{4,12},{5,13},{6,14},{7,15},{8,0},{9,1},... | collective-permute-start | bytes 200 | tf_op jit(solution)/shard_map/ppermute | solution.py:38
  332.8 14.1 %collective-permute-start.37 = (f32[16]{0:T(128)S(1)}, f32[16]{0:T(128)S(1)}, u32[]{:S(2)}, u32[]{:S(2)}) collective-permute-start(f32[16]{0:T(128)S(1)} %add.265), channel_id=1, source_target_pairs={{0,16},{1,17},{2,18},{3,19},{4,20},{5,21},{6,22},{7,23},{8,24},{9,... | collective-permute-start | bytes 200 | tf_op jit(solution)/shard_map/ppermute | solution.py:38
  347.0 5.4 %collective-permute-start.38 = (f32[16]{0:T(128)S(1)}, f32[16]{0:T(128)S(1)}, u32[]{:S(2)}, u32[]{:S(2)}) collective-permute-start(f32[16]{0:T(128)S(1)} %add.266), channel_id=1, source_target_pairs={{0,32},{32,0},{64,96},{96,64},{128,160},{160,128},{192,224},{224,1... | collective-permute-start | bytes 200 | tf_op jit(solution)/shard_map/ppermute | solution.py:38
  352.4 6.9 %collective-permute-start.39 = (f32[16]{0:T(128)S(1)}, f32[16]{0:T(128)S(1)}, u32[]{:S(2)}, u32[]{:S(2)}) collective-permute-start(f32[16]{0:T(128)S(1)} %add.267), channel_id=1, source_target_pairs={{0,64},{32,96},{64,0},{96,32},{128,192},{160,224},{192,128},{224,1... | collective-permute-start | bytes 200 | tf_op jit(solution)/shard_map/ppermute | solution.py:38
  359.3 5.4 %collective-permute-start.40 = (f32[16]{0:T(128)S(1)}, f32[16]{0:T(128)S(1)}, u32[]{:S(2)}, u32[]{:S(2)}) collective-permute-start(f32[16]{0:T(128)S(1)} %add.268), channel_id=1, source_target_pairs={{0,128},{32,160},{64,192},{96,224},{128,0},{160,32},{192,64},{224,... | collective-permute-start | bytes 200 | tf_op jit(solution)/shard_map/ppermute | solution.py:38
  364.8 6.9 %collective-permute-start.41 = (f32[16]{0:T(128)S(1)}, f32[16]{0:T(128)S(1)}, u32[]{:S(2)}, u32[]{:S(2)}) collective-permute-start(f32[16]{0:T(128)S(1)} %add.269), channel_id=1, source_target_pairs={{0,256},{32,288},{64,320},{96,352},{128,384},{160,416},{192,448},{... | collective-permute-start | bytes 200 | tf_op jit(solution)/shard_map/ppermute | solution.py:38
  (23 other events, 154.6 us)
